TPU v7x, 256 devices: a whole 4x4x8 slice. The times are simulated.
256 devices in a mesh: dp: 8 (over x, core), seq: 32 (over y, z).
Axes of the slice: x: 4, y: 4, z: 8, core: 2. Of those that a mesh axis runs over, the one named last changes fastest.
Arguments:
- voxels: bfloat16 [8, 4096, 4096], P('dp', 'seq'), may hold values from -6 to 6
- patch_weight: bfloat16 [4096, 1024], replicated, may hold values from -0.09375 to 0.09375
- patch_bias: float32 [1024], replicated, may hold values from -3 to 3
- enc_position: bfloat16 [4096, 1024], P('seq'), may hold values from -5 to 5
- visible: int32 [8, 4096], P('dp', 'seq'), may hold values from 0 to 1, as said below
- enc_project: bfloat16 [1024, 3072], P(('dp', 'seq')), may hold values from -1 to 1
- enc_merge: bfloat16 [1024, 1024], P(('dp', 'seq')), may hold values from -0.1875 to 0.1875
- dec_lift: bfloat16 [1024, 512], P(('dp', 'seq')), may hold values from -0.1875 to 0.1875
- mask_token: float32 [512], replicated, may hold values from -4 to 4
- dec_position: bfloat16 [4096, 512], P('seq'), may hold values from -5 to 5
- dec_project: bfloat16 [512, 1536], P(('dp', 'seq')), may hold values from -1 to 1
- dec_merge: bfloat16 [512, 512], P(('dp', 'seq')), may hold values from -0.25 to 0.25
- dec_predict: bfloat16 [512, 4096], P(('dp', 'seq')), may hold values from -0.25 to 0.25
Outputs:
- decoded: bfloat16 [8, 4096, 512], P('dp', 'seq')
- patch_loss: float32 [8, 4096], P('dp', 'seq')
Inputs may be any that keep to these rules, and one draw needn't show every extreme that they name: `visible`: each cube has exactly 1024 ones. Each slab of 128 consecutive patches holds between 0 and 64 ones, and in every cube some slab holds exactly 64.
All inputs are finite; a program needn't handle non-finite values.
Results may differ from a plain program's by a relative error of at most 0.008.
Values may be sent and summed in bfloat16 or wider, within the bound.
No kernel may reach another device: no remote copies, remote signals or barrier semaphores. Data moves between devices by JAX's collectives and lax.ppermute only.
A program may use at most 128 MiB of HBM per device.

v0:
```python
import math
import jax
import jax.numpy as jnp
from jax import lax
from jax.sharding import PartitionSpec as P

ENC_HEADS = 16
DEC_HEADS = 16


def layer_norm(values):
    centre = values - jnp.mean(values, axis=-1, keepdims=True)
    spread = jnp.mean(centre * centre, axis=-1, keepdims=True)
    return centre * lax.rsqrt(spread + 1e-06)


def attend_rows(queries, key_rows, value_rows, key_ok):
    query_rows, local_heads, head_size = queries.shape
    block_rows = math.gcd(query_rows, 512)
    score_scale = 1.0 / math.sqrt(head_size)
    query_blocks = queries[:, 0].reshape(query_rows // block_rows, block_rows, head_size)
    keys_one = key_rows[:, 0]
    values_one = value_rows[:, 0]

    def one_block(query_block):
        scores = (
            jnp.einsum("qd,kd->qk", query_block, keys_one, preferred_element_type=jnp.float32)
            * score_scale
        )
        if key_ok is not None:
            scores = jnp.where(key_ok[None, :], scores, -1e30)
        top_score = jnp.max(scores, axis=-1, keepdims=True)
        exponent = jnp.exp(scores - top_score)
        weights = (exponent / jnp.sum(exponent, axis=-1, keepdims=True)).astype(jnp.bfloat16)
        return jnp.einsum(
            "qk,kd->qd", weights, values_one, preferred_element_type=jnp.float32
        ).astype(jnp.bfloat16)

    head_outputs = [lax.map(one_block, query_blocks).reshape(query_rows, head_size)]
    return jnp.stack(head_outputs, axis=1)


def spread_heads(packed, heads, seq_count):
    row_count = packed.shape[0]
    head_size = packed.shape[1] // (3 * heads)
    query_parts = max(seq_count // heads, 1)
    local_heads = max(heads // seq_count, 1)
    layout = packed.reshape(row_count, 3, heads, head_size)
    layout = jnp.repeat(layout, query_parts, axis=2)
    layout = layout.reshape(row_count, 3, seq_count, local_heads, head_size).transpose(
        2, 1, 0, 3, 4
    )
    return layout.reshape(seq_count, 3, row_count, local_heads * head_size)


def attend_heads(incoming, key_ok, heads, query_part, query_parts):
    sources, _, row_count, piece_width = incoming.shape
    local_heads = max(heads // sources, 1)
    head_size = piece_width // local_heads
    all_rows = sources * row_count
    thirds = [incoming[:, third].reshape(all_rows, local_heads, head_size) for third in range(3)]
    query_rows = all_rows // query_parts
    queries = lax.dynamic_slice_in_dim(thirds[0], query_part * query_rows, query_rows, 0)
    return attend_rows(queries, thirds[1], thirds[2], key_ok)


def place_rows(mixed_part, all_rows, query_part, sources):
    query_rows = mixed_part.shape[0]
    flat_part = mixed_part.reshape(query_rows, -1)
    buffer = jnp.zeros((all_rows, flat_part.shape[1]), jnp.bfloat16)
    buffer = lax.dynamic_update_slice(buffer, flat_part, (query_part * query_rows, 0))
    return buffer.reshape(sources, all_rows // sources, flat_part.shape[1])


def collect_heads(returned, heads, query_parts):
    sources, row_count, piece_width = returned.shape
    local_heads = max(heads // sources, 1)
    head_size = piece_width // local_heads
    arranged = returned.reshape(sources, row_count, local_heads, head_size).transpose(1, 0, 2, 3)
    arranged = arranged.reshape(row_count, heads, query_parts, head_size)
    summed = jnp.sum(arranged.astype(jnp.float32), axis=2).astype(jnp.bfloat16)
    return summed.reshape(row_count, heads * head_size)


def send_blocks(packed, heads, seq_count):
    row_count = packed.shape[0]
    head_size = packed.shape[1] // (3 * heads)
    query_parts = seq_count // heads
    part_rows = row_count // query_parts
    layout = packed.reshape(row_count, 3, heads, head_size)
    queries = layout[:, 0].reshape(query_parts, part_rows, heads, head_size).transpose(2, 0, 1, 3)
    queries = queries.reshape(seq_count, 1, part_rows, head_size)
    pairs = (
        layout[:, 1:].transpose(2, 1, 0, 3).reshape(heads, 2 * query_parts, part_rows, head_size)
    )
    pairs = jnp.broadcast_to(pairs[:, None], (heads, query_parts) + pairs.shape[1:])
    pairs = pairs.reshape(seq_count, 2 * query_parts, part_rows, head_size)
    return jnp.concatenate([queries, pairs], axis=1)


def attend_blocks(incoming, key_ok):
    sources, blocks, part_rows, head_size = incoming.shape
    query_parts = (blocks - 1) // 2
    queries = incoming[:, 0].reshape(sources * part_rows, 1, head_size)
    keys = incoming[:, 1 : 1 + query_parts].reshape(-1, 1, head_size)
    values = incoming[:, 1 + query_parts :].reshape(-1, 1, head_size)
    mixed = attend_rows(queries, keys, values, key_ok)
    return mixed.reshape(sources, part_rows, head_size)


def take_blocks(returned, heads):
    seq_count, part_rows, head_size = returned.shape
    query_parts = seq_count // heads
    arranged = returned.reshape(heads, query_parts, part_rows, head_size).transpose(1, 2, 0, 3)
    return arranged.reshape(query_parts * part_rows, heads * head_size)


def gather_weights(pieces):
    flat = jnp.concatenate([piece.reshape(-1) for piece in pieces])
    every = lax.all_gather(flat, ("dp", "seq"), axis=0, tiled=True)
    lane = 128
    sources = every.shape[0] // flat.shape[0]
    tiles = every.reshape(sources, flat.shape[0] // lane, lane)
    wholes = []
    start = 0
    for piece in pieces:
        size = piece.size
        part = tiles[:, start // lane : (start + size) // lane, :]
        wholes.append(part.reshape(sources * piece.shape[0], piece.shape[1]))
        start += size
    return wholes


def weight_dot(rows, weight):
    return jnp.dot(rows, weight, preferred_element_type=jnp.float32)


def shards(
    voxels,
    patch_weight,
    patch_bias,
    enc_position,
    visible,
    enc_project,
    enc_merge,
    dec_lift,
    mask_token,
    dec_position,
    dec_project,
    dec_merge,
    dec_predict,
):
    seq_count = lax.axis_size("seq")
    seq_place = lax.axis_index("seq")
    enc_parts = max(seq_count // ENC_HEADS, 1)
    dec_parts = max(seq_count // DEC_HEADS, 1)
    enc_part = seq_place % enc_parts
    dec_part = seq_place % dec_parts
    project_rows, project_width = enc_project.shape
    tile_rows = 2 * project_rows
    partner = lax.ppermute(
        enc_project, "seq", perm=[(place, place ^ 1) for place in range(seq_count)]
    )
    half = seq_place % 2
    tile_block = jnp.where(
        half == 0,
        jnp.concatenate([enc_project, partner], axis=0),
        jnp.concatenate([partner, enc_project], axis=0),
    )
    own_width = project_width // 2
    own_block = lax.dynamic_slice_in_dim(tile_block, half * own_width, own_width, axis=1)
    own_block = (
        own_block.reshape(tile_rows, own_width // 128, 128).transpose(1, 0, 2).reshape(-1, 128)
    )
    tiled_project, full_merge, full_lift, *dec_weights = gather_weights(
        (own_block, enc_merge, dec_lift, dec_project, dec_merge, dec_predict)
    )
    full_project = (
        tiled_project.reshape(-1, 2, own_width // 128, tile_rows, 128)
        .transpose(0, 3, 1, 2, 4)
        .reshape(-1, project_width)
    )
    tok_local = voxels.shape[1]
    slab_max = tok_local // 2
    slot_ids = jnp.arange(slab_max, dtype=jnp.int32)
    cube_index = 0
    cube_flags = visible[cube_index]
    embedded = (
        jnp.dot(voxels[cube_index], patch_weight, preferred_element_type=jnp.float32)
        + patch_bias
        + enc_position.astype(jnp.float32)
    ).astype(jnp.bfloat16)
    ranking = jnp.cumsum(cube_flags) - 1
    slot_index = jnp.where(cube_flags == 1, ranking, slab_max)
    chooser = (slot_index[None, :] == slot_ids[:, None]).astype(jnp.bfloat16)
    kept_rows = jnp.dot(chooser, embedded, preferred_element_type=jnp.float32).astype(jnp.bfloat16)
    present = slot_ids < jnp.sum(cube_flags)
    packed = weight_dot(
        layer_norm(kept_rows.astype(jnp.float32)).astype(jnp.bfloat16), full_project
    ).astype(jnp.bfloat16)
    key_marks = jnp.broadcast_to(present.astype(jnp.bfloat16)[None, :], (seq_count, slab_max))
    outgoing = send_blocks(packed, ENC_HEADS, seq_count)
    incoming = lax.all_to_all(outgoing, "seq", split_axis=0, concat_axis=0, tiled=True)
    incoming, full_merge, full_lift, dec_weights[0] = lax.optimization_barrier(
        (incoming, full_merge, full_lift, dec_weights[0])
    )
    in_marks = lax.all_to_all(key_marks, "seq", split_axis=0, concat_axis=0, tiled=True)
    key_ok = in_marks.reshape(-1) > 0.5
    returning = attend_blocks(incoming, key_ok)
    returned = lax.all_to_all(returning, "seq", split_axis=0, concat_axis=0, tiled=True)
    mixed_rows = take_blocks(returned, ENC_HEADS)
    encoded = kept_rows.astype(jnp.float32) + weight_dot(mixed_rows, full_merge)
    lifted_list = [weight_dot(layer_norm(encoded).astype(jnp.bfloat16), full_lift)]
    rank_list = [ranking]
    cube_index = 0
    cube_flags = visible[cube_index]
    taken_rows = jnp.take(
        lifted_list[cube_index], jnp.clip(rank_list[cube_index], 0, slab_max - 1), axis=0
    )
    dec_in = (
        jnp.where(cube_flags[:, None] == 1, taken_rows, mask_token[None, :])
        + dec_position.astype(jnp.float32)
    ).astype(jnp.bfloat16)
    dec_packed = weight_dot(
        layer_norm(dec_in.astype(jnp.float32)).astype(jnp.bfloat16), dec_weights[0]
    ).astype(jnp.bfloat16)
    outgoing = send_blocks(dec_packed, DEC_HEADS, seq_count)
    incoming = lax.all_to_all(outgoing, "seq", split_axis=0, concat_axis=0, tiled=True)
    incoming, dec_weights[1], dec_weights[2] = lax.optimization_barrier(
        (incoming, dec_weights[1], dec_weights[2])
    )
    returning = attend_blocks(incoming, None)
    returned = lax.all_to_all(returning, "seq", split_axis=0, concat_axis=0, tiled=True)
    mixed_rows = take_blocks(returned, DEC_HEADS)
    decoded = (dec_in.astype(jnp.float32) + weight_dot(mixed_rows, dec_weights[1])).astype(
        jnp.bfloat16
    )
    predicted = weight_dot(
        layer_norm(decoded.astype(jnp.float32)).astype(jnp.bfloat16), dec_weights[2]
    )
    target = layer_norm(voxels[cube_index].astype(jnp.float32))
    squared = jnp.mean((predicted - target) * (predicted - target), axis=-1)
    loss_list = [jnp.where(cube_flags == 1, jnp.zeros_like(squared), squared)]
    decoded_list = [decoded]
    return (jnp.stack(decoded_list), jnp.stack(loss_list))


def solution(mesh):
    return jax.shard_map(
        shards,
        mesh=mesh,
        in_specs=(
            P("dp", "seq", None),
            P(),
            P(),
            P("seq", None),
            P("dp", "seq"),
            P(("dp", "seq"), None),
            P(("dp", "seq"), None),
            P(("dp", "seq"), None),
            P(),
            P("seq", None),
            P(("dp", "seq"), None),
            P(("dp", "seq"), None),
            P(("dp", "seq"), None),
        ),
        out_specs=(P("dp", "seq", None), P("dp", "seq")),
        check_vma=False,
    )
```

profile of v0, /device:TPU:32, one launch (start us, length us, event | category | flops | bytes accessed | tf_op | source)
XLA Modules:
  0.0 296.1 jit_solution(1052979018624724954)
XLA Ops:
  7.2 1.9 collective-permute-start
  11.9 0.9 fusion.60
  14.2 0.8 copy.52
  15.8 1.3 fusion.67
  18.4 10.7 %all-to-all-start = ((bf16[32,1,64]{2,1,0:T(2,128)(2,1)}), bf16[32,1,64]{2,1,0:T(2,128)(2,1)S(1)}, u32[]{:S(2)}, u32[]{:S(2)}) async-start(bf16[32,1,64]{2,1,0:T(2,128)(2,1)} %broadcast_in_dim.99), calls=%async_computation | async-start | bytes 32768 | tf_op jit(solution)/shard_map/all_to_all | solution.py:207
  29.2 5.2 %fusion.68 = (f32[64]{0:T(128)S(1)}, f32[64,1024]{1,0:T(8,128)S(1)}) fusion(bf16[4096,1024]{1,0:T(8,128)(2,1)} %param.18, bf16[1,128,4096]{2,1,0:T(8,128)(2,1)} %param.17, bf16[128,1024]{1,0:T(8,128)(2,1)} %param.20, f32[1024]{0:T(1024)} %param.19, s32[128]{0:T(128)S(1)} %get-tuple-element.118), kind=kOutput, calls=%fused_computation.125 | convolution fusion | flops 1091248128 | bytes 9966336 | tf_op jit(solution)/shard_map/dot_general | solution.py:196
  34.6 105.6 %all-gather.2.cloned.1.call-done = bf16[7864320]{0:T(1024)(128)(2,1)} async-done(((bf16[30720]{0:T(1024)(128)(2,1)}), bf16[7864320]{0:T(1024)(128)(2,1)}) %all-gather.2.cloned.1.call-update) | async-done | bytes 15728656 | tf_op jit(solution)/shard_map/all_gather | solution.py:120
  140.1 4.0 %slice.66 = bf16[256,96,128]{2,1,0:T(8,128)(2,1)S(1)} slice(bf16[256,240,128]{2,1,0:T(8,128)(2,1)} %bitcast.143), slice={[0:256], [0:96], [0:128]} | slice | bytes 12582912 | tf_op jit(solution)/shard_map/slice | solution.py:128
  144.1 1.3 convolution_convert_fusion
  146.8 1.6 reshape.253
  148.3 7.4 %all-to-all-start.1 = ((bf16[32,2,5120]{2,1,0:T(2,128)(2,1)}), bf16[32,2,5120]{2,1,0:T(2,128)(2,1)S(1)}, u32[]{:S(2)}, u32[]{:S(2)}) async-start(bf16[32,2,5120]{2,1,0:T(2,128)(2,1)} %reshape.253), calls=%async_computation.1 | async-start | bytes 1310720 | tf_op jit(solution)/shard_map/all_to_all | solution.py:203
  155.8 1.2 fusion.64
  157.2 3.3 %slice.69 = bf16[256,32,128]{2,1,0:T(8,128)(2,1)} slice(bf16[256,240,128]{2,1,0:T(8,128)(2,1)} %bitcast.144), slice={[0:256], [96:128], [0:128]} | slice | bytes 4194304 | tf_op jit(solution)/shard_map/slice | solution.py:128
  160.5 2.9 slice.71
  163.4 2.4 slice.70
  165.8 2.8 reshape.229
  168.6 4.3 %reshape.231 = bf16[512,1536]{1,0:T(8,128)(2,1)} reshape(bf16[256,24,128]{2,1,0:T(8,128)(2,1)} %slice.71) | data formatting | bytes 3145728 | tf_op jit(solution)/shard_map/reshape | solution.py:129
  172.9 2.5 reshape.230
  175.4 1.1 all-to-all-done.1
  176.5 1.8 reshape.254
  178.4 2.1 fusion.66
  180.4 1.0 slice.54
  181.4 7.4 %while.20 = (s32[]{:T(128)}, bf16[2,512,64]{1,2,0:T(8,128)(2,1)}, pred[2048]{0:T(1024)(128)(4,1)S(1)}, bf16[2,512,64]{2,1,0:T(8,128)(2,1)S(1)}, bf16[2048,64]{1,...) while((s32[]{:T(128)}, bf16[2,512,64]{1,2,0:T(8,128)(2,1)}, pred[2048]{0:T(1024)(128)(4,1)S(1)}, ...), condition=%wide.region_7.8_spmd, body=%wide.region_4.7_spmd.sunk | while | flops 281050112 | bytes 15941801 | solution.py:39
  181.5 0.8 fusion.97
  182.3 0.9 fusion.98
  183.2 1.3 fusion.99
  185.2 0.8 fusion.97
  186.0 0.9 fusion.98
  186.9 1.3 fusion.99
  188.8 1.1 copy.55
  189.9 0.9 reshape.255
  190.8 8.8 %all-to-all-start.2 = ((bf16[32,2,1024]{2,1,0:T(2,128)(2,1)}), bf16[32,2,1024]{2,1,0:T(2,128)(2,1)S(1)}, u32[]{:S(2)}, u32[]{:S(2)}) async-start(bf16[32,2,1024]{2,1,0:T(2,128)(2,1)} %reshape.255), calls=%async_computation.2 | async-start | bytes 262144 | tf_op jit(solution)/shard_map/all_to_all | solution.py:210
  199.6 9.7 %all-to-all-done.2 = bf16[32,2,1024]{2,1,0:T(2,128)(2,1)S(1)} async-done(((bf16[32,2,1024]{2,1,0:T(2,128)(2,1)}), bf16[32,2,1024]{2,1,0:T(2,128)(2,1)S(1)}, u32[]{:S(2)}, u32[]{:S(2)}) %all-to-all-start.2) | async-done | bytes 131104 | tf_op jit(solution)/shard_map/all_to_all | solution.py:210
  210.7 1.7 fusion.45
  212.4 0.8 gather_fusion
  216.1 1.5 reshape.257
  217.6 4.4 %all-to-all-start.3 = ((bf16[32,2,5120]{2,1,0:T(2,128)(2,1)}), bf16[32,2,5120]{2,1,0:T(2,128)(2,1)S(1)}, u32[]{:S(2)}, u32[]{:S(2)}) async-start(bf16[32,2,5120]{2,1,0:T(2,128)(2,1)} %reshape.257), calls=%async_computation.3 | async-start | bytes 1310720 | tf_op jit(solution)/shard_map/all_to_all | solution.py:228
  222.2 5.2 %slice.75 = bf16[256,64,128]{2,1,0:T(8,128)(2,1)} slice(bf16[256,240,128]{2,1,0:T(8,128)(2,1)} %bitcast.147), slice={[0:256], [176:240], [0:128]} | slice | bytes 8388608 | tf_op jit(solution)/shard_map/slice | solution.py:128
  227.4 1.1 slice.74
  228.5 7.3 %reshape.238 = bf16[512,4096]{1,0:T(8,128)(2,1)} reshape(bf16[256,64,128]{2,1,0:T(8,128)(2,1)} %slice.75) | data formatting | bytes 8388608 | tf_op jit(solution)/shard_map/reshape | solution.py:129
  236.1 5.2 %all-to-all-done.3 = bf16[32,2,5120]{2,1,0:T(2,128)(2,1)S(1)} async-done(((bf16[32,2,5120]{2,1,0:T(2,128)(2,1)}), bf16[32,2,5120]{2,1,0:T(2,128)(2,1)S(1)}, u32[]{:S(2)}, u32[]{:S(2)}) %all-to-all-start.3) | async-done | bytes 655392 | tf_op jit(solution)/shard_map/all_to_all | solution.py:228
  241.3 0.7 reshape.258
  242.0 0.9 fusion.65
  243.0 0.7 slice.61
  243.7 1.5 copy.71
  245.2 1.3 copy.72
  246.6 1.2 copy.70
  247.8 20.5 %while.21 = (s32[]{:T(128)}, bf16[4,512,32]{1,2,0:T(8,128)(2,1)S(1)}, bf16[4,512,32]{2,1,0:T(8,128)(2,1)S(1)}, bf16[4096,32]{1,0:T(8,128)(2,1)S(1)}, bf16[4096,32]{1,0:T(8,128)(2,1)}, /*index=5*/s32[]{:T(128)}) while((s32[]{:T(128)}, bf16[4,512,32]{1,2,0:T(8,128)(2,1)S(1)}, bf16[4,512,32]{2,1,0:T(8,128)(2,1)S(1)}, ...), condition=%wide.region_15.16_spmd, body=%wide.region_12.15_spmd.sunk | while | flops 287325184 | bytes 28485736 | solution.py:39
  247.8 1.3 multiply_reduce_fusion.4
  249.2 1.5 fusion.102
  250.7 2.3 fusion.103
  252.9 1.3 multiply_reduce_fusion.4
  254.3 1.5 fusion.102
  255.8 2.3 fusion.103
  258.1 1.3 multiply_reduce_fusion.4
  259.4 1.5 fusion.102
  260.9 2.3 fusion.103
  263.2 1.3 multiply_reduce_fusion.4
  264.6 1.5 fusion.102
  266.1 2.3 fusion.103
  268.8 0.8 reshape.259
  269.6 4.9 %all-to-all-start.4 = ((bf16[32,2,1024]{2,1,0:T(2,128)(2,1)}), bf16[32,2,1024]{2,1,0:T(2,128)(2,1)S(1)}, u32[]{:S(2)}, u32[]{:S(2)}) async-start(bf16[32,2,1024]{2,1,0:T(2,128)(2,1)} %reshape.259), calls=%async_computation.4 | async-start | bytes 262144 | tf_op jit(solution)/shard_map/all_to_all | solution.py:233
  274.9 9.2 %all-to-all-done.4 = bf16[32,2,1024]{2,1,0:T(2,128)(2,1)S(1)} async-done(((bf16[32,2,1024]{2,1,0:T(2,128)(2,1)}), bf16[32,2,1024]{2,1,0:T(2,128)(2,1)S(1)}, u32[]{:S(2)}, u32[]{:S(2)}) %all-to-all-start.4) | async-done | bytes 131104 | tf_op jit(solution)/shard_map/all_to_all | solution.py:233
  285.3 3.4 %fusion.26 = f32[128]{0:T(128)S(1)} fusion(bf16[512,4096]{1,0:T(8,128)(2,1)} %reshape.238, bf16[1,128,4096]{2,1,0:T(8,128)(2,1)S(1)} %copy-done, f32[128]{0:T(128)S(1)} %get-tuple-element.125, f32[128]{0:T(128)S(1)} %broadcast_multiply_fusion, bf16[128,512]{1,0:T(8,128)(2,1)S(1)} %get-tuple-element.124, f32[128]{0:T(128)S(1)} %get-tuple-element.126, ...), kind=kOutput, calls=%fused_computation.38 | convolution fusion | flops 540278656 | bytes 5376512 | tf_op jit(solution)/shard_map/dot_general | solution.py:135
  (116 shorter events, 16.6 us)
Async XLA Ops:
  7.2 133.0 %all-gather.2.cloned.1.call-start = ((), (), s32[]{:S(2)}) async-start(), calls=%async_computation.5 | async-start | bytes 15790080 | tf_op jit(solution)/shard_map/all_gather | solution.py:120
  7.2 4.7 %collective-permute-start = (bf16[4,3072]{1,0:T(4,128)(2,1)}, bf16[4,3072]{1,0:T(4,128)(2,1)S(1)}, u32[]{:S(2)}, u32[]{:S(2)}) collective-permute-start(bf16[4,3072]{1,0:T(4,128)(2,1)} %param.22), channel_id=1, source_target_pairs={{0,1},{1,0},{2,3},{3,2},{4,5},{5,4},{6,7},{7,6},{8,9},{9,8},{10,11... | collective-permute-start | bytes 73736 | tf_op jit(solution)/shard_map/ppermute | solution.py:161
  13.5 0.6 copy-start.11
  18.4 129.9 %all-to-all-start = ((bf16[32,1,64]{2,1,0:T(2,128)(2,1)}), bf16[32,1,64]{2,1,0:T(2,128)(2,1)S(1)}, u32[]{:S(2)}, u32[]{:S(2)}) async-start(bf16[32,1,64]{2,1,0:T(2,128)(2,1)} %broadcast_in_dim.99), calls=%async_computation | async-start | bytes 32768 | tf_op jit(solution)/shard_map/all_to_all | solution.py:207
  148.3 28.2 %all-to-all-start.1 = ((bf16[32,2,5120]{2,1,0:T(2,128)(2,1)}), bf16[32,2,5120]{2,1,0:T(2,128)(2,1)S(1)}, u32[]{:S(2)}, u32[]{:S(2)}) async-start(bf16[32,2,5120]{2,1,0:T(2,128)(2,1)} %reshape.253), calls=%async_computation.1 | async-start | bytes 1310720 | tf_op jit(solution)/shard_map/all_to_all | solution.py:203
  181.4 18.2 %copy-start.13 = (s32[128]{0:T(128)S(1)}, s32[128]{0:T(128)}, u32[]{:S(2)}) copy-start(s32[128]{0:T(128)} %get-tuple-element.84) | copy-start | bytes 1540
  181.4 18.2 %copy-start.15 = (s32[128]{0:T(128)S(1)}, s32[128]{0:T(128)}, u32[]{:S(2)}) copy-start(s32[128]{0:T(128)} %get-tuple-element.82) | copy-start | bytes 1540
  181.5 1.8 copy-start.6
  181.5 1.8 copy-start.8
  184.5 0.7 copy-start.9
  185.2 1.7 copy-start.6
  185.2 1.7 copy-start.8
  188.2 0.7 copy-start.9
  190.8 22.4 %copy-start.7 = (bf16[128,512]{1,0:T(8,128)(2,1)S(1)}, bf16[128,512]{1,0:T(8,128)(2,1)}, u32[]{:S(2)}) copy-start(bf16[128,512]{1,0:T(8,128)(2,1)} %param.26) | copy-start | bytes 393220
  190.8 22.4 %copy-start.12 = (f32[512]{0:T(512)S(1)}, f32[512]{0:T(512)}, u32[]{:S(2)}) copy-start(f32[512]{0:T(512)} %param.25) | copy-start | bytes 6148
  190.8 22.4 %copy-start.16 = (pred[128]{0:T(512)(128)(4,1)S(1)}, pred[128]{0:T(512)(128)(4,1)}, u32[]{:S(2)}) copy-start(pred[128]{0:T(512)(128)(4,1)} %fusion.64) | copy-start | bytes 388
  190.8 18.5 %all-to-all-start.2 = ((bf16[32,2,1024]{2,1,0:T(2,128)(2,1)}), bf16[32,2,1024]{2,1,0:T(2,128)(2,1)S(1)}, u32[]{:S(2)}, u32[]{:S(2)}) async-start(bf16[32,2,1024]{2,1,0:T(2,128)(2,1)} %reshape.255), calls=%async_computation.2 | async-start | bytes 262144 | tf_op jit(solution)/shard_map/all_to_all | solution.py:210
  210.5 3.5 %copy-start.1 = (bf16[512,1536]{1,0:T(8,128)(2,1)S(1)}, bf16[512,1536]{1,0:T(8,128)(2,1)}, u32[]{:S(2)}) copy-start(bf16[512,1536]{1,0:T(8,128)(2,1)} %reshape.231) | copy-start | bytes 4718596
  213.4 0.7 copy-start.2
  215.4 6.6 %copy-start = (bf16[1,128,4096]{2,1,0:T(8,128)(2,1)S(1)}, bf16[1,128,4096]{2,1,0:T(8,128)(2,1)}, u32[]{:S(2)}) copy-start(bf16[1,128,4096]{2,1,0:T(8,128)(2,1)} %param.17) | copy-start | bytes 3145732
  217.6 23.6 %all-to-all-start.3 = ((bf16[32,2,5120]{2,1,0:T(2,128)(2,1)}), bf16[32,2,5120]{2,1,0:T(2,128)(2,1)S(1)}, u32[]{:S(2)}, u32[]{:S(2)}) async-start(bf16[32,2,5120]{2,1,0:T(2,128)(2,1)} %reshape.257), calls=%async_computation.3 | async-start | bytes 1310720 | tf_op jit(solution)/shard_map/all_to_all | solution.py:228
  242.0 5.8 %copy-start.10 = (bf16[4,512,32]{1,2,0:T(8,128)(2,1)S(1)}, bf16[4,512,32]{1,2,0:T(8,128)(2,1)}, u32[]{:S(2)}) copy-start(bf16[4,512,32]{1,2,0:T(8,128)(2,1)} %custom-call.4) | copy-start | bytes 393220
  249.1 1.5 copy-start.4
  254.3 1.5 copy-start.4
  259.4 1.5 copy-start.4
  264.5 1.5 copy-start.4
  268.3 16.4 %copy-start.3 = (bf16[128,512]{1,0:T(8,128)(2,1)S(1)}, bf16[128,512]{1,0:T(8,128)(2,1)}, u32[]{:S(2)}) copy-start(bf16[128,512]{1,0:T(8,128)(2,1)} %copy-done.2) | copy-start | bytes 393220
  269.6 14.5 %all-to-all-start.4 = ((bf16[32,2,1024]{2,1,0:T(2,128)(2,1)}), bf16[32,2,1024]{2,1,0:T(2,128)(2,1)S(1)}, u32[]{:S(2)}, u32[]{:S(2)}) async-start(bf16[32,2,1024]{2,1,0:T(2,128)(2,1)} %reshape.259), calls=%async_computation.4 | async-start | bytes 262144 | tf_op jit(solution)/shard_map/all_to_all | solution.py:233
  285.1 3.6 %copy-start.5 = (bf16[128,512]{1,0:T(8,128)(2,1)}, bf16[128,512]{1,0:T(8,128)(2,1)S(1)}, u32[]{:S(2)}) copy-start(bf16[128,512]{1,0:T(8,128)(2,1)S(1)} %get-tuple-element.124) | copy-start | bytes 393220
  285.3 3.4 %copy-start.14 = (s32[1,128]{1,0:T(1,128)S(1)}, s32[1,128]{1,0:T(1,128)}, u32[]{:S(2)}) copy-start(s32[1,128]{1,0:T(1,128)} %param.21) | copy-start | bytes 1540
Sparse Core Ops, SparseCore 0:
  14.3 125.7 all-gather.1
where the time goes:
time: 298 us; the launch traced here: 296 us
  waiting for transfers between devices  131 us (44%)
  local copies, waits for them, and re-layouts  65.5 us (22%)
  starting transfers between devices  38.1 us (13%)
  matrix products  31.4 us (11%)
  other arithmetic  15.6 us (5%)
  between operations  14.6 us (5%)
    all_gather x1, waiting for transfers between devices, gather_weights(): every = lax.all_gather(flat, ('dp', 'seq'), axis=0, tiled=True)  106 us
    all_to_all x2, waiting for transfers between devices, shards(): lax.all_to_all(returning, 'seq', split_axis=0, concat_axis=0, tiled=True)  18.9 us
    slice x6, local copies, waits for them, and re-layouts, gather_weights(): part = tiles[:, start // lane:(start + size) // lane, :]  18.8 us
    reshape x5, local copies, waits for them, and re-layouts, gather_weights(): wholes.append(part.reshape(sources * piece.shape[0], piece.shape[1]))  17.2 us
    all_to_all x2, starting transfers between devices, shards(): lax.all_to_all(returning, 'seq', split_axis=0, concat_axis=0, tiled=True)  13.6 us
    all_to_all x2, starting transfers between devices, shards(): lax.all_to_all(outgoing, 'seq', split_axis=0, concat_axis=0, tiled=True)  11.8 us
    dot_general x6, matrix products, one_block(): jnp.einsum('qk,kd->qd', weights, values_one, preferred_element_type=jnp.f...  11.6 us
    all_to_all x1, starting transfers between devices, shards(): lax.all_to_all(key_marks, 'seq', split_axis=0, concat_axis=0, tiled=True)  10.7 us
  transfers between devices with their start and end apart: 7, of which 5 were waited for; matrix products, arithmetic and copies ran while one was open for 18% of the time, Pallas kernels for 0%

commit v1 on v0

--- a/solution.py
+++ b/solution.py
@@ -117,7 +117,8 @@
 
 def gather_weights(pieces):
     flat = jnp.concatenate([piece.reshape(-1) for piece in pieces])
-    every = lax.all_gather(flat, ("dp", "seq"), axis=0, tiled=True)
+    sent = jnp.stack([flat] * lax.axis_size(("dp", "seq")))
+    every = jnp.concatenate(lax.all_to_all(sent, ("dp", "seq"), 0, 0), axis=0)
     lane = 128
     sources = every.shape[0] // flat.shape[0]
     tiles = every.reshape(sources, flat.shape[0] // lane, lane)

time: 298 us -> 836 us (2.81); the launches traced: 296 us -> 823 us
  waiting for transfers between devices: 131 us -> 355 us
  local copies, waits for them, and re-layouts: 65.5 us -> 263 us
  other arithmetic: 15.6 us -> 107 us
  starting transfers between devices: 38.1 us -> 57.5 us
  between operations: 14.6 us -> 1.59 us
    all_to_all x0 -> x1, waiting for transfers between devices: none -> 336 us  [gather_weights(): every = jnp.concatenate(lax.all_to_all(sent, ('dp', 'seq'), 0, 0), axis=0)]
    all_gather x1 -> x0, waiting for transfers between devices: 106 us -> none  [gather_weights(): every = lax.all_gather(flat, ('dp', 'seq'), axis=0, tiled=True)]
    another operation x1 -> x2, other arithmetic: 0.17 us -> 94 us  [the longest x1 93.8 us: gather_weights(): sent = jnp.stack([flat] * lax.axis_size(('dp', 'seq')))]
    unnamed x41 -> x37, local copies, waits for them, and re-layouts: 10.1 us -> 103 us
    all_to_all x0 -> x1, local copies, waits for them, and re-layouts: none -> 60.5 us  [gather_weights(): every = jnp.concatenate(lax.all_to_all(sent, ('dp', 'seq'), 0, 0), axis=0)]
    slice x6 -> x12, local copies, waits for them, and re-layouts: 18.8 us -> 44 us  [gather_weights(): part = tiles[:, start // lane:(start + size) // lane, :]]
    another operation x0 -> x2, local copies, waits for them, and re-layouts: none -> 19.1 us  [gather_weights(): sent = jnp.stack([flat] * lax.axis_size(('dp', 'seq')))]
    all_to_all x0 -> x1, starting transfers between devices: none -> 14.7 us  [gather_weights(): every = jnp.concatenate(lax.all_to_all(sent, ('dp', 'seq'), 0, 0), axis=0)]
  transfers between devices with their start and end apart: 7 -> 7, of which waited for: 5 -> 3; matrix products, arithmetic and copies ran while one was open for 18% -> 26% of each run, Pallas kernels for 0% -> 0%
where the time goes in v1:
time: 836 us; the launch traced here: 823 us
  waiting for transfers between devices  355 us (42%)
  local copies, waits for them, and re-layouts  263 us (31%)
  other arithmetic  107 us (13%)
  starting transfers between devices  57.5 us (7%)
  matrix products  38 us (5%)
    all_to_all x1, waiting for transfers between devices, gather_weights(): every = jnp.concatenate(lax.all_to_all(sent, ('dp', 'seq'), 0, 0), axis=0)  336 us
    unnamed x37, local copies, waits for them, and re-layouts  103 us
    another operation x1, other arithmetic, gather_weights(): sent = jnp.stack([flat] * lax.axis_size(('dp', 'seq')))  93.8 us
    all_to_all x1, local copies, waits for them, and re-layouts, gather_weights(): every = jnp.concatenate(lax.all_to_all(sent, ('dp', 'seq'), 0, 0), axis=0)  60.5 us
    slice x12, local copies, waits for them, and re-layouts, gather_weights(): part = tiles[:, start // lane:(start + size) // lane, :]  44 us
    all_to_all x2, starting transfers between devices, shards(): lax.all_to_all(returning, 'seq', split_axis=0, concat_axis=0, tiled=True)  20.1 us
    reshape x5, local copies, waits for them, and re-layouts, gather_weights(): wholes.append(part.reshape(sources * piece.shape[0], piece.shape[1]))  19.3 us
    another operation x2, local copies, waits for them, and re-layouts, gather_weights(): sent = jnp.stack([flat] * lax.axis_size(('dp', 'seq')))  19.1 us
  transfers between devices with their start and end apart: 7, of which 3 were waited for; matrix products, arithmetic and copies ran while one was open for 26% of the time, Pallas kernels for 0%

profile of v1, /device:TPU:32, one launch (start us, length us, event | category | flops | bytes accessed | tf_op | source)
XLA Modules:
  0.0 822.8 jit_solution(6684544895241375536)
XLA Ops:
  0.6 1.9 collective-permute-start
  5.4 0.9 fusion.60
  7.0 18.6 %stack.4 = bf16[256,1,30720]{2,1,0:T(2,128)(2,1)} broadcast(bf16[30720]{0:T(1024)(128)(2,1)S(1)} %constant_dynamic-update-slice_fusion), dimensions={2} | broadcast | bytes 15790080 | tf_op jit(solution)/shard_map/stack | solution.py:120
  26.1 93.8 %reduce.9 = bf16[256,30720]{1,0:T(8,128)(2,1)} reduce(bf16[256,1,30720]{2,1,0:T(2,128)(2,1)} %stack.4, bf16[]{:T(256)} %broadcast.272), dimensions={1}, to_apply=%stack.4.reduce_sub_computation | reduce | bytes 31457282 | tf_op jit(solution)/shard_map/stack | solution.py:120
  119.9 20.1 %reshape.257 = bf16[256,2,15360]{2,1,0:T(2,128)(2,1)} reshape(bf16[256,30720]{1,0:T(8,128)(2,1)} %reduce.9) | data formatting | bytes 31457280
  140.0 14.7 %all-to-all-start.1 = ((bf16[256,2,15360]{2,1,0:T(2,128)(2,1)}), bf16[256,2,15360]{2,1,0:T(2,128)(2,1)}, u32[]{:S(2)}, u32[]{:S(2)}) async-start(bf16[256,2,15360]{2,1,0:T(2,128)(2,1)} %reshape.257), calls=%async_computation.1 | async-start | bytes 31457280 | tf_op jit(solution)/shard_map/all_to_all | solution.py:121
  156.4 4.9 fusion.68
  161.5 336.4 %all-to-all-done.1 = bf16[256,2,15360]{2,1,0:T(2,128)(2,1)} async-done(((bf16[256,2,15360]{2,1,0:T(2,128)(2,1)}), bf16[256,2,15360]{2,1,0:T(2,128)(2,1)}, u32[]{:S(2)}, u32[]{:S(2)}) %all-to-all-start.1) | async-done | bytes 15728672 | tf_op jit(solution)/shard_map/all_to_all | solution.py:121
  498.6 6.5 all-to-all-start
  505.1 73.9 %reshape.258 = bf16[256,1,30720]{2,1,0:T(2,128)(2,1)} reshape(bf16[256,2,15360]{2,1,0:T(2,128)(2,1)} %all-to-all-done.1) | data formatting | bytes 31457280
  579.0 60.5 %copy.66 = bf16[256,1,30720]{0,2,1:T(8,128)(2,1)} copy(bf16[256,1,30720]{2,1,0:T(2,128)(2,1)} %reshape.258) | data formatting | bytes 31457280 | tf_op jit(solution)/shard_map/all_to_all | solution.py:121
  639.6 6.2 slice.66
  645.8 8.9 %copy.67 = bf16[256,96,128]{2,1,0:T(8,128)(2,1)} copy(bf16[256,96,128]{0,2,1:T(8,128)(2,1)} %slice.66) | data formatting | bytes 12582912 | tf_op jit(solution)/shard_map/slice | solution.py:129
  654.7 4.0 convolution_convert_fusion
  660.1 1.6 reshape.259
  661.7 9.8 %all-to-all-start.2 = ((bf16[32,2,5120]{2,1,0:T(2,128)(2,1)}), bf16[32,2,5120]{2,1,0:T(2,128)(2,1)}, u32[]{:S(2)}, u32[]{:S(2)}) async-start(bf16[32,2,5120]{2,1,0:T(2,128)(2,1)} %reshape.259), calls=%async_computation.2 | async-start | bytes 1310720 | tf_op jit(solution)/shard_map/all_to_all | solution.py:204
  671.7 3.2 slice.69
  674.9 2.7 slice.71
  677.6 1.3 slice.70
  678.9 4.6 copy.70
  683.5 4.2 reshape.233
  687.7 2.8 copy.72
  690.4 4.3 reshape.235
  694.7 1.8 copy.71
  696.5 2.5 reshape.234
  699.0 2.5 reshape.260
  701.5 1.0 fusion.66
  702.5 6.1 while.20
  703.3 0.9 fusion.98
  704.3 1.3 fusion.99
  706.4 0.9 fusion.98
  707.3 1.3 fusion.99
  709.6 10.2 %all-to-all-start.3 = ((bf16[32,2,1024]{2,1,0:T(2,128)(2,1)}), bf16[32,2,1024]{2,1,0:T(2,128)(2,1)S(1)}, u32[]{:S(2)}, u32[]{:S(2)}) async-start(bf16[32,2,1024]{2,1,0:T(2,128)(2,1)} %reshape.261), calls=%async_computation.3 | async-start | bytes 262144 | tf_op jit(solution)/shard_map/all_to_all | solution.py:211
  719.9 9.5 %all-to-all-done.3 = bf16[32,2,1024]{2,1,0:T(2,128)(2,1)S(1)} async-done(((bf16[32,2,1024]{2,1,0:T(2,128)(2,1)}), bf16[32,2,1024]{2,1,0:T(2,128)(2,1)S(1)}, u32[]{:S(2)}, u32[]{:S(2)}) %all-to-all-start.3) | async-done | bytes 131104 | tf_op jit(solution)/shard_map/all_to_all | solution.py:211
  730.0 2.2 fusion.71
  734.0 1.8 convolution_convert_fusion.1
  737.4 1.6 reshape.263
  739.1 4.5 all-to-all-start.4
  743.8 4.6 slice.75
  748.4 1.1 slice.74
  749.5 6.6 copy.80
  756.0 7.3 reshape.242
  763.7 1.1 reshape.241
  765.6 1.2 fusion.65
  767.5 1.5 copy.91
  769.0 2.4 copy.92
  771.4 1.2 copy.90
  772.6 23.0 %while.21 = (s32[]{:T(128)}, bf16[4,512,32]{1,2,0:T(8,128)(2,1)}, bf16[4,512,32]{2,1,0:T(8,128)(2,1)S(1)}, bf16[4096,32]{1,0:T(8,128)(2,1)S(1)}, bf16[4096,32]{1,0:T(8,128)(2,1)}, /*index=5*/s32[]{:T(128)}) while((s32[]{:T(128)}, bf16[4,512,32]{1,2,0:T(8,128)(2,1)}, bf16[4,512,32]{2,1,0:T(8,128)(2,1)S(1)}, bf16[4096,32]{1,0:T(8,128)(2,1)S(1)}, ...), condition=%wide.region_15.16_spmd, body=%wide.region_12.15_spmd.sunk | while | flops 287325184 | bytes 27699812 | solution.py:39
  772.6 1.3 multiply_reduce_fusion.4
  773.9 1.5 fusion.102
  775.4 2.9 fusion.103
  778.3 1.3 multiply_reduce_fusion.4
  779.7 1.5 fusion.102
  781.2 2.9 fusion.103
  784.1 1.3 multiply_reduce_fusion.4
  785.4 1.5 fusion.102
  786.9 2.9 fusion.103
  789.8 1.3 multiply_reduce_fusion.4
  791.1 1.5 fusion.102
  792.7 2.9 fusion.103
  795.5 1.1 copy.87
  797.8 9.9 %all-to-all-start.5 = ((bf16[32,2,1024]{2,1,0:T(2,128)(2,1)}), bf16[32,2,1024]{2,1,0:T(2,128)(2,1)S(1)}, u32[]{:S(2)}, u32[]{:S(2)}) async-start(bf16[32,2,1024]{2,1,0:T(2,128)(2,1)} %reshape.265), calls=%async_computation.5 | async-start | bytes 262144 | tf_op jit(solution)/shard_map/all_to_all | solution.py:234
  808.1 9.2 %all-to-all-done.5 = bf16[32,2,1024]{2,1,0:T(2,128)(2,1)S(1)} async-done(((bf16[32,2,1024]{2,1,0:T(2,128)(2,1)}), bf16[32,2,1024]{2,1,0:T(2,128)(2,1)S(1)}, u32[]{:S(2)}, u32[]{:S(2)}) %all-to-all-start.5) | async-done | bytes 131104 | tf_op jit(solution)/shard_map/all_to_all | solution.py:234
  818.5 3.4 fusion.26
  (113 shorter events, 19.8 us)
Async XLA Ops:
  0.6 4.7 collective-permute-start
  140.0 14.7 %copy-start.10 = (s32[1,128]{1,0:T(1,128)S(1)}, s32[1,128]{1,0:T(1,128)}, u32[]{:S(2)}) copy-start(s32[1,128]{1,0:T(1,128)} %param.21) | copy-start | bytes 1540
  140.0 16.4 %copy-start = (bf16[1,128,4096]{2,1,0:T(8,128)(2,1)S(1)}, bf16[1,128,4096]{2,1,0:T(8,128)(2,1)}, u32[]{:S(2)}) copy-start(bf16[1,128,4096]{2,1,0:T(8,128)(2,1)} %param.17) | copy-start | bytes 3145732
  140.0 16.4 %copy-start.6 = (bf16[128,1024]{1,0:T(8,128)(2,1)S(1)}, bf16[128,1024]{1,0:T(8,128)(2,1)}, u32[]{:S(2)}) copy-start(bf16[128,1024]{1,0:T(8,128)(2,1)} %param.20) | copy-start | bytes 786436
  140.0 16.4 %copy-start.8 = (f32[1024]{0:T(1024)S(1)}, f32[1024]{0:T(1024)}, u32[]{:S(2)}) copy-start(f32[1024]{0:T(1024)} %param.19) | copy-start | bytes 12292
  140.0 358.0 %all-to-all-start.1 = ((bf16[256,2,15360]{2,1,0:T(2,128)(2,1)}), bf16[256,2,15360]{2,1,0:T(2,128)(2,1)}, u32[]{:S(2)}, u32[]{:S(2)}) async-start(bf16[256,2,15360]{2,1,0:T(2,128)(2,1)} %reshape.257), calls=%async_computation.1 | async-start | bytes 31457280 | tf_op jit(solution)/shard_map/all_to_all | solution.py:121
  498.6 163.1 %all-to-all-start = ((bf16[32,1,64]{2,1,0:T(2,128)(2,1)}), bf16[32,1,64]{2,1,0:T(2,128)(2,1)S(1)}, u32[]{:S(2)}, u32[]{:S(2)}) async-start(bf16[32,1,64]{2,1,0:T(2,128)(2,1)} %broadcast_in_dim.99), calls=%async_computation | async-start | bytes 32768 | tf_op jit(solution)/shard_map/all_to_all | solution.py:208
  661.7 37.3 %all-to-all-start.2 = ((bf16[32,2,5120]{2,1,0:T(2,128)(2,1)}), bf16[32,2,5120]{2,1,0:T(2,128)(2,1)}, u32[]{:S(2)}, u32[]{:S(2)}) async-start(bf16[32,2,5120]{2,1,0:T(2,128)(2,1)} %reshape.259), calls=%async_computation.2 | async-start | bytes 1310720 | tf_op jit(solution)/shard_map/all_to_all | solution.py:204
  702.5 1.7 copy-start.5
  705.5 1.8 copy-start.5
  708.6 23.9 %copy-start.1 = (bf16[1024,512]{1,0:T(8,128)(2,1)S(1)}, bf16[1024,512]{1,0:T(8,128)(2,1)}, u32[]{:S(2)}) copy-start(bf16[1024,512]{1,0:T(8,128)(2,1)} %reshape.234) | copy-start | bytes 3145732
  709.6 23.9 %copy-start.7 = (bf16[128,512]{1,0:T(8,128)(2,1)S(1)}, bf16[128,512]{1,0:T(8,128)(2,1)}, u32[]{:S(2)}) copy-start(bf16[128,512]{1,0:T(8,128)(2,1)} %param.26) | copy-start | bytes 393220
  709.6 23.9 %copy-start.9 = (f32[512]{0:T(512)S(1)}, f32[512]{0:T(512)}, u32[]{:S(2)}) copy-start(f32[512]{0:T(512)} %param.25) | copy-start | bytes 6148
  709.6 19.8 %all-to-all-start.3 = ((bf16[32,2,1024]{2,1,0:T(2,128)(2,1)}), bf16[32,2,1024]{2,1,0:T(2,128)(2,1)S(1)}, u32[]{:S(2)}, u32[]{:S(2)}) async-start(bf16[32,2,1024]{2,1,0:T(2,128)(2,1)} %reshape.261), calls=%async_computation.3 | async-start | bytes 262144 | tf_op jit(solution)/shard_map/all_to_all | solution.py:211
  739.1 25.7 %all-to-all-start.4 = ((bf16[32,2,5120]{2,1,0:T(2,128)(2,1)}), bf16[32,2,5120]{2,1,0:T(2,128)(2,1)S(1)}, u32[]{:S(2)}, u32[]{:S(2)}) async-start(bf16[32,2,5120]{2,1,0:T(2,128)(2,1)} %reshape.263), calls=%async_computation.4 | async-start | bytes 1310720 | tf_op jit(solution)/shard_map/all_to_all | solution.py:229
  773.9 1.5 copy-start.3
  779.7 1.5 copy-start.3
  785.4 1.5 copy-start.3
  791.1 1.5 copy-start.3
  795.5 22.4 %copy-start.2 = (bf16[512,512]{1,0:T(8,128)(2,1)S(1)}, bf16[512,512]{1,0:T(8,128)(2,1)}, u32[]{:S(2)}) copy-start(bf16[512,512]{1,0:T(8,128)(2,1)} %reshape.241) | copy-start | bytes 1572868
  797.8 19.6 %all-to-all-start.5 = ((bf16[32,2,1024]{2,1,0:T(2,128)(2,1)}), bf16[32,2,1024]{2,1,0:T(2,128)(2,1)S(1)}, u32[]{:S(2)}, u32[]{:S(2)}) async-start(bf16[32,2,1024]{2,1,0:T(2,128)(2,1)} %reshape.265), calls=%async_computation.5 | async-start | bytes 262144 | tf_op jit(solution)/shard_map/all_to_all | solution.py:234
  818.3 3.6 copy-start.4
  818.5 3.4 copy-start.11
